TPU v7x, 256 devices: a whole 4x4x8 slice. The times are simulated.
256 devices in a mesh: feat: 32 (over y, x, core), samp: 8 (over z).
Axes of the slice: x: 4, y: 4, z: 8, core: 2. Of those that a mesh axis runs over, the one named last changes fastest.
Arguments:
- hash_codes: int32 [32, 6144, 1024], P('feat', 'samp'), may hold values from 0 to 4095
- sample_index: int32 [32, 65536], P('feat', 'samp'), may hold values from 0 to 767, as said below
- labels: int32 [8192, 8], P('feat', 'samp'), may hold values 0 or 1
- encoder_first: bfloat16 [32, 1024, 2048], P('feat'), may hold values from -0.1875 to 0.1875
- encoder_second: bfloat16 [32, 2048, 256], P('feat'), may hold values from -0.125 to 0.125
- top_weight: bfloat16 [1024, 1024], replicated, may hold values from -0.1875 to 0.1875
- score_vector: bfloat16 [1024], replicated, may hold values from -0.1875 to 0.1875
Outputs:
- row_grads: float32 [32, 6144, 256], P('feat', 'samp')
- grad_first: float32 [32, 1024, 2048], P('feat', 'samp')
- grad_second: float32 [32, 2048, 256], P('feat', 'samp')
Inputs may be any that keep to these rules, and one draw needn't show every extreme that they name: `sample_index`: for each feature and sample group the slots used by the group's 8192 samples are 0 to some count minus 1, each at least once; for some feature and group that count is 768.
All inputs are finite; a program needn't handle non-finite values. No bound on the sum of `labels` on one device may be relied on, other than what follows from the above.
Results may differ from a plain program's by a relative error of at most 0.019.
Values may be sent and summed in bfloat16 or wider, within the bound.
No kernel may reach another device: no remote copies, remote signals or barrier semaphores. Data moves between devices by JAX's collectives and lax.ppermute only.
A program may use at most 128 MiB of HBM per device.

v0:
```python
import jax
import jax.numpy as jnp
from jax import lax
from jax.sharding import PartitionSpec as P

BUCKETS = 4096
loss_scale = 256.0


def silu_slope(inputs):
    logistic = jax.nn.sigmoid(inputs)
    return logistic * (1.0 + inputs * (1.0 - logistic))


def top_tower(picked, label_block, top_weight, score_vector):
    feats, count, width = picked.shape
    pair_dots = (
        jnp.einsum("fne,hne->nfh", picked, picked, preferred_element_type=jnp.float32)
        * width ** (-0.5)
    ).astype(jnp.bfloat16)
    pair_flat = pair_dots.reshape(count, feats * feats)
    top_pre = jnp.dot(pair_flat, top_weight, preferred_element_type=jnp.float32)
    top_hidden = jax.nn.silu(top_pre).astype(jnp.bfloat16)
    logits = jnp.dot(top_hidden, score_vector, preferred_element_type=jnp.float32)
    dlogit = loss_scale * (jax.nn.sigmoid(logits) - label_block.astype(jnp.float32))
    top_delta = (
        dlogit[:, None] * score_vector.astype(jnp.float32)[None, :] * silu_slope(top_pre)
    ).astype(jnp.bfloat16)
    pair_delta = jnp.einsum(
        "nk,jk->nj", top_delta, top_weight, preferred_element_type=jnp.float32
    ).reshape(count, feats, feats)
    pair_sym = (pair_delta + jnp.swapaxes(pair_delta, 1, 2)).astype(jnp.bfloat16)
    emb_delta = jnp.einsum(
        "nfh,hne->fne", pair_sym, picked, preferred_element_type=jnp.float32
    ) * width ** (-0.5)
    return emb_delta.astype(jnp.bfloat16)


def local(
    hash_codes, sample_index, labels, encoder_first, encoder_second, top_weight, score_vector
):
    feat_count = lax.axis_size("feat")
    encoded = (hash_codes[0].astype(jnp.float32) * (2.0 / (BUCKETS - 1)) - 1.0).astype(jnp.bfloat16)
    first_pre = jnp.dot(encoded, encoder_first[0], preferred_element_type=jnp.float32)
    first_hidden = jax.nn.silu(first_pre).astype(jnp.bfloat16)
    row_table = jnp.dot(first_hidden, encoder_second[0], preferred_element_type=jnp.float32).astype(
        jnp.bfloat16
    )
    positions = sample_index[0]
    slot_count = row_table.shape[0]
    emb_width = row_table.shape[1]
    chosen_rows = jnp.take(row_table, positions, axis=0).reshape(feat_count, -1, emb_width)
    picked = lax.all_to_all(chosen_rows, "feat", split_axis=0, concat_axis=0, tiled=True)
    emb_delta = top_tower(picked, labels[:, 0], top_weight, score_vector)
    returned = lax.all_to_all(emb_delta, "feat", split_axis=0, concat_axis=0, tiled=True)
    row_grads = jax.ops.segment_sum(
        returned.reshape(-1, emb_width).astype(jnp.float32), positions, num_segments=slot_count
    )
    row_delta = row_grads.astype(jnp.bfloat16)
    second_local = jnp.einsum(
        "rk,re->ke", first_hidden, row_delta, preferred_element_type=jnp.float32
    )
    first_back = jnp.einsum(
        "re,ke->rk", row_delta, encoder_second[0], preferred_element_type=jnp.float32
    )
    first_delta = (first_back * silu_slope(first_pre)).astype(jnp.bfloat16)
    first_local = jnp.einsum("rh,rk->hk", encoded, first_delta, preferred_element_type=jnp.float32)
    total_first, total_second = (
        lax.psum(first_local.astype(jnp.bfloat16), "samp").astype(jnp.float32),
        lax.psum(second_local.astype(jnp.bfloat16), "samp").astype(jnp.float32),
    )
    shard_id = lax.axis_index("samp")
    group_count = lax.axis_size("samp")
    first_rows = total_first.shape[0] // group_count
    second_rows = total_second.shape[0] // group_count
    share_first = lax.dynamic_slice_in_dim(total_first, shard_id * first_rows, first_rows, 0)
    share_second = lax.dynamic_slice_in_dim(total_second, shard_id * second_rows, second_rows, 0)
    return (row_grads[None], share_first[None], share_second[None])


def solution(mesh):
    return jax.shard_map(
        local,
        mesh=mesh,
        in_specs=(
            P("feat", "samp", None),
            P("feat", "samp"),
            P("feat", "samp"),
            P("feat", None, None),
            P("feat", None, None),
            P(),
            P(),
        ),
        out_specs=(P("feat", "samp", None), P("feat", "samp", None), P("feat", "samp", None)),
        check_vma=False,
    )
```

profile of v0, /device:TPU:1, one launch (start us, length us, event | category | flops | bytes accessed | tf_op | source)
XLA Modules:
  0.0 400.1 jit_solution(6173155816172626765)
XLA Ops:
  7.2 0.0 copy-start
  7.2 0.9 compare_select_fusion
  8.1 0.5 broadcast.66
  8.7 1.5 reduce.3
  10.2 0.0 copy-start.5
  10.2 9.8 %multiply_convert_fusion.2 = (bf16[768,2048]{1,0:T(8,128)(2,1)S(1)}, f32[768,2048]{1,0:T(8,128)}) fusion(bf16[1,1024,2048]{2,1,0:T(8,128)(2,1)} %param.10, s32[1,768,1024]{2,1,0:T(8,128)} %param.7), kind=kOutput, calls=%fused_computation.6 | convolution fusion | flops 3232235520 | bytes 16777216 | tf_op jit(solution)/shard_map/dot_general | solution.py:44
  20.0 1.6 copy-done.6
  21.7 1.0 convolution_convert_fusion.2
  22.7 33.1 %gather_fusion = bf16[8192,256]{1,0:T(8,128)(2,1)} fusion(bf16[768,256]{1,0:T(8,128)(2,1)S(1)} %convolution_convert_fusion.2, s32[8192]{0:T(1024)S(1)} %broadcast_clamp_fusion), kind=kCustom, calls=%fused_computation | custom fusion | bytes 8421376 | tf_op jit(solution)/shard_map/jit(_take)/gather | solution.py:52
  55.7 5.2 %broadcast_select_fusion = bf16[32,256,256]{2,1,0:T(8,128)(2,1)} fusion(bf16[32,256,256]{2,1,0:T(8,128)(2,1)} %bitcast.47, pred[32,256]{1,0:T(8,128)(4,1)S(1)} %compare_and_fusion), kind=kLoop, calls=%fused_computation.11 | loop fusion | flops 2097152 | bytes 8396800 | tf_op jit(solution)/shard_map/jit(_take)/select_n | solution.py:52
  61.0 8.8 %all-to-all-start = ((bf16[32,256,256]{2,1,0:T(8,128)(2,1)}), bf16[32,256,256]{2,1,0:T(8,128)(2,1)}, u32[]{:S(2)}, u32[]{:S(2)}) async-start(bf16[32,256,256]{2,1,0:T(8,128)(2,1)} %broadcast_select_fusion), calls=%async_computation | async-start | bytes 8388608 | tf_op jit(solution)/shard_map/all_to_all | solution.py:53
  69.8 0.0 all-reduce.3.cloned.1.call-start
  69.9 50.2 %all-to-all-done = bf16[32,256,256]{2,1,0:T(8,128)(2,1)} async-done(((bf16[32,256,256]{2,1,0:T(8,128)(2,1)}), bf16[32,256,256]{2,1,0:T(8,128)(2,1)}, u32[]{:S(2)}, u32[]{:S(2)}) %all-to-all-start) | async-done | bytes 4194336 | tf_op jit(solution)/shard_map/all_to_all | solution.py:53
  120.0 10.2 %fusion.5 = f32[256,32,32]{2,1,0:T(8,128)} fusion(bf16[32,256,256]{2,1,0:T(8,128)(2,1)} %all-to-all-done), kind=kOutput, calls=%fused_computation.13 | convolution fusion | flops 134217728 | bytes 5242880 | tf_op jit(solution)/shard_map/fne,hne->nfh/dot_general | solution.py:18
  130.2 3.5 copy.33
  133.8 0.1 multiply_convert_fusion.5
  133.9 0.7 fusion.35
  134.6 0.4 fusion.20
  135.0 1.0 fusion.16
  136.0 0.6 fusion.12
  136.6 3.0 copy.37
  139.7 4.9 %fusion.2 = bf16[32,256,256]{2,0,1:T(8,128)(2,1)S(1)} fusion(bf16[256,32,32]{2,1,0:T(8,128)(2,1)S(1)} %copy.37, bf16[32,256,256]{2,1,0:T(8,128)(2,1)} %all-to-all-done), kind=kOutput, calls=%fused_computation.8 | convolution fusion | flops 138412032 | bytes 8912896 | tf_op jit(solution)/shard_map/nfh,hne->fne/dot_general | solution.py:33
  144.6 2.4 copy.38
  147.0 57.9 %all_to_all.10 = bf16[32,256,256]{2,1,0:T(8,128)(2,1)} all-to-all(bf16[32,256,256]{2,1,0:T(8,128)(2,1)S(1)} %copy.38), channel_id=1, replica_groups=mesh['feat'=32,'samp'=8] {'feat'}, dimensions={0} | all-to-all | bytes 8388608 | tf_op jit(solution)/shard_map/all_to_all | solution.py:55
  204.9 40.9 %scatter_custom_fusion = f32[768,256]{1,0:T(8,128)S(1)} fusion(s32[8192]{0:T(1024)} %bitcast.51, bf16[8192,256]{1,0:T(8,128)(2,1)} %bitcast.46, f32[]{:T(128)} %constant.15.clone.1), kind=kCustom, calls=%fused_computation.2 | custom fusion | flops 4194304 | bytes 4981248 | tf_op jit(solution)/shard_map/scatter-add | solution.py:56
  245.9 0.0 copy-start.2
  245.9 4.2 %convolution_convert_fusion.1 = bf16[2048,256]{1,0:T(8,128)(2,1)} fusion(bf16[768,2048]{1,0:T(8,128)(2,1)} %copy-done.6, f32[768,256]{1,0:T(8,128)S(1)} %scatter_custom_fusion), kind=kOutput, calls=%fused_computation.18 | convolution fusion | flops 806027264 | bytes 4980736 | tf_op jit(solution)/shard_map/rk,re->ke/dot_general | solution.py:60
  250.1 10.4 %convolution_convert_fusion = bf16[1024,2048]{1,0:T(8,128)(2,1)} fusion(f32[768,2048]{1,0:T(8,128)} %get-tuple-element.6, bf16[1,2048,256]{2,1,0:T(8,128)(2,1)} %param.11, s32[1,768,1024]{2,1,0:T(8,128)} %param.7, f32[768,256]{1,0:T(8,128)S(1)} %scatter_custom_fusion), kind=kOutput, calls=%fused_computation.12 | convolution fusion | flops 4046127104 | bytes 15466496 | tf_op jit(solution)/shard_map/rh,rk->hk/dot_general | solution.py:67
  260.5 0.0 all-reduce.3.cloned.1.call-update
  260.5 129.0 %all-reduce.3.cloned.1.call-done = (bf16[1024,2048]{1,0:T(8,128)(2,1)}, bf16[2048,256]{1,0:T(8,128)(2,1)}) async-done(((bf16[1024,2048]{1,0:T(8,128)(2,1)}, bf16[2048,256]{1,0:T(8,128)(2,1)}), (bf16[1024,2048]{1,0:T(8,128)(2,1)}, bf16[2048,256]{1,0:T(8,128)(2,1)})) %all-reduce.3.cloned.1.call-update) | async-done | bytes 5242896 | tf_op jit(solution)/shard_map/psum | solution.py:69
  389.5 2.1 convert_bitcast_fusion
  391.6 1.6 convert_bitcast_fusion.1
  (17 shorter events, 0.1 us)
Async XLA Ops:
  7.2 126.7 %copy-start = (bf16[1024,1024]{1,0:T(8,128)(2,1)S(1)}, bf16[1024,1024]{1,0:T(8,128)(2,1)}, u32[]{:S(2)}) copy-start(bf16[1024,1024]{1,0:T(8,128)(2,1)} %param.12) | copy-start | bytes 6291460
  10.2 11.5 %copy-start.5 = (bf16[1,2048,256]{2,1,0:T(8,128)(2,1)S(1)}, bf16[1,2048,256]{2,1,0:T(8,128)(2,1)}, u32[]{:S(2)}) copy-start(bf16[1,2048,256]{2,1,0:T(8,128)(2,1)} %param.11) | copy-start | bytes 3145732
  20.0 1.6 copy-start.6
  61.0 8.8 %copy-start.3 = (bf16[1024]{0:T(1024)(128)(2,1)S(1)}, bf16[1024]{0:T(1024)(128)(2,1)}, u32[]{:S(2)}) copy-start(bf16[1024]{0:T(1024)(128)(2,1)} %param.13) | copy-start | bytes 6148
  61.0 8.9 %copy-start.4 = (s32[256,1]{0,1:T(1,128)S(1)}, s32[256,1]{0,1:T(1,128)}, u32[]{:S(2)}) copy-start(s32[256,1]{0,1:T(1,128)} %param.9) | copy-start | bytes 3076
  61.0 59.0 %all-to-all-start = ((bf16[32,256,256]{2,1,0:T(8,128)(2,1)}), bf16[32,256,256]{2,1,0:T(8,128)(2,1)}, u32[]{:S(2)}, u32[]{:S(2)}) async-start(bf16[32,256,256]{2,1,0:T(8,128)(2,1)} %broadcast_select_fusion), calls=%async_computation | async-start | bytes 8388608 | tf_op jit(solution)/shard_map/all_to_all | solution.py:53
  69.8 319.7 %all-reduce.3.cloned.1.call-start = ((), (), s32[]{:S(2)}) async-start(), calls=%async_computation.2 | async-start | bytes 10485760 | tf_op jit(solution)/shard_map/psum | solution.py:69
  245.9 4.2 %copy-start.2 = (f32[768,256]{1,0:T(8,128)}, f32[768,256]{1,0:T(8,128)S(1)}, u32[]{:S(2)}) copy-start(f32[768,256]{1,0:T(8,128)S(1)} %scatter_custom_fusion) | copy-start | bytes 2359300
  250.1 143.2 %copy-start.1 = (bf16[1024,1024]{1,0:T(8,128)(2,1)S(1)}, bf16[1024,1024]{1,0:T(8,128)(2,1)}, u32[]{:S(2)}) copy-start(bf16[1024,1024]{1,0:T(8,128)(2,1)} %param.12) | copy-start | bytes 6291460
Sparse Core Ops, SparseCore 0:
  260.6 128.8 all-reduce.2
where the time goes:
time: 401 us; the launch traced here: 400 us
  waiting for transfers between devices  179 us (45%)
  blocking collectives  57.9 us (14%)
  other arithmetic  53.1 us (13%)
  local copies, waits for them, and re-layouts  44.2 us (11%)
  matrix products  42.7 us (11%)
  between operations  14.2 us (4%)
  starting transfers between devices  8.82 us (2%)
    psum x1, waiting for transfers between devices, local(): lax.psum(first_local.astype(jnp.bfloat16), 'samp').astype(jnp.float32)  129 us
    all_to_all x1, blocking collectives, local(): lax.all_to_all(emb_delta, 'feat', split_axis=0, concat_axis=0, tiled=True)  57.9 us
    all_to_all x1, waiting for transfers between devices, local(): lax.all_to_all(chosen_rows, 'feat', split_axis=0, concat_axis=0, tiled=True)  50.2 us
    scatter-add x1, other arithmetic, local(): jax.ops.segment_sum(returned.reshape(-1, emb_width).astype(jnp.float32),...  40.9 us
    gather x1, local copies, waits for them, and re-layouts, local(): jnp.take(row_table, positions, axis=0).reshape(feat_count, -1, emb_width)  33.1 us
    dot_general x1, matrix products, local(): jnp.einsum('rh,rk->hk', encoded, first_delta, preferred_element_type=jnp....  10.4 us
    dot_general x1, matrix products, top_tower(): jnp.einsum('fne,hne->nfh', picked, picked, preferred_element_type=jnp.flo...  10.2 us
    dot_general x1, matrix products, local(): jnp.dot(encoded, encoder_first[0], preferred_element_type=jnp.float32)  9.85 us
  transfers between devices with their start and end apart: 2, of which 2 were waited for; matrix products, arithmetic and copies ran while one was open for 0% of the time, Pallas kernels for 0%

commit v1 on v0

--- a/solution.py
+++ b/solution.py
@@ -66,7 +66,9 @@
     first_delta = (first_back * silu_slope(first_pre)).astype(jnp.bfloat16)
     first_local = jnp.einsum("rh,rk->hk", encoded, first_delta, preferred_element_type=jnp.float32)
     total_first, total_second = (
-        lax.psum(first_local.astype(jnp.bfloat16), "samp").astype(jnp.float32),
+        jnp.sum(lax.all_gather(first_local.astype(jnp.bfloat16), "samp"), axis=0).astype(
+            jnp.float32
+        ),
         lax.psum(second_local.astype(jnp.bfloat16), "samp").astype(jnp.float32),
     )
     shard_id = lax.axis_index("samp")

time: 401 us -> 680 us (1.70)
  waiting for transfers between devices: 179 us -> 444 us
  other arithmetic: 53.1 us -> 67.4 us
    all_gather x0 -> x1, waiting for transfers between devices: none -> 333 us  [local(): lax.all_gather(first_local.astype(jnp.bfloat16), 'samp')]
    psum x1, waiting for transfers between devices: 129 us -> 61.5 us  [local(): lax.psum(second_local.astype(jnp.bfloat16), 'samp').astype(jnp.float32)]
    reduce_sum x0 -> x1, other arithmetic: none -> 14.3 us  [local(): jnp.sum(lax.all_gather(first_local.astype(jnp.bfloat16), 'samp'), axis=0)]
  transfers between devices with their start and end apart: 2 -> 3, of which waited for: 2 -> 3; matrix products, arithmetic and copies ran while one was open for 0% -> 2% of each run, Pallas kernels for 0% -> 0%
where the time goes in v1:
time: 680 us; the launch traced here: 679 us
  waiting for transfers between devices  444 us (65%)
  other arithmetic  67.4 us (10%)
  blocking collectives  57.9 us (9%)
  local copies, waits for them, and re-layouts  44.1 us (6%)
  matrix products  42.4 us (6%)
  between operations  14.2 us (2%)
  starting transfers between devices  8.86 us (1%)
    all_gather x1, waiting for transfers between devices, local(): lax.all_gather(first_local.astype(jnp.bfloat16), 'samp')  333 us
    psum x1, waiting for transfers between devices, local(): lax.psum(second_local.astype(jnp.bfloat16), 'samp').astype(jnp.float32)  61.5 us
    all_to_all x1, blocking collectives, local(): lax.all_to_all(emb_delta, 'feat', split_axis=0, concat_axis=0, tiled=True)  57.9 us
    all_to_all x1, waiting for transfers between devices, local(): lax.all_to_all(chosen_rows, 'feat', split_axis=0, concat_axis=0, tiled=True)  50.2 us
    scatter-add x1, other arithmetic, local(): jax.ops.segment_sum(returned.reshape(-1, emb_width).astype(jnp.float32),...  40.9 us
    gather x1, local copies, waits for them, and re-layouts, local(): jnp.take(row_table, positions, axis=0).reshape(feat_count, -1, emb_width)  33 us
    reduce_sum x1, other arithmetic, local(): jnp.sum(lax.all_gather(first_local.astype(jnp.bfloat16), 'samp'), axis=0)  14.3 us
  transfers between devices with their start and end apart: 3, of which 3 were waited for; matrix products, arithmetic and copies ran while one was open for 2% of the time, Pallas kernels for 0%

profile of v1, /device:TPU:1, one launch (start us, length us, event | category | flops | bytes accessed | tf_op | source)
XLA Modules:
  0.0 679.3 jit_solution(8447596960640439455)
XLA Ops:
  7.2 0.9 compare_select_fusion
  8.1 0.5 broadcast.66
  8.7 1.5 reduce.4
  10.2 9.8 %multiply_convert_fusion.2 = (bf16[768,2048]{1,0:T(8,128)(2,1)S(1)}, f32[768,2048]{1,0:T(8,128)}) fusion(bf16[1,1024,2048]{2,1,0:T(8,128)(2,1)} %param.10, s32[1,768,1024]{2,1,0:T(8,128)} %param.7), kind=kOutput, calls=%fused_computation.6 | convolution fusion | flops 3232235520 | bytes 16777216 | tf_op jit(solution)/shard_map/dot_general | solution.py:44
  20.0 1.6 copy-done.7
  21.7 1.0 convolution_convert_fusion.2
  22.7 33.0 %gather_fusion = bf16[8192,256]{1,0:T(8,128)(2,1)} fusion(bf16[768,256]{1,0:T(8,128)(2,1)S(1)} %convolution_convert_fusion.2, s32[8192]{0:T(1024)S(1)} %broadcast_clamp_fusion), kind=kCustom, calls=%fused_computation | custom fusion | bytes 8421376 | tf_op jit(solution)/shard_map/jit(_take)/gather | solution.py:52
  55.6 5.2 broadcast_select_fusion
  60.9 8.8 %all-to-all-start = ((bf16[32,256,256]{2,1,0:T(8,128)(2,1)}), bf16[32,256,256]{2,1,0:T(8,128)(2,1)}, u32[]{:S(2)}, u32[]{:S(2)}) async-start(bf16[32,256,256]{2,1,0:T(8,128)(2,1)} %broadcast_select_fusion), calls=%async_computation | async-start | bytes 8388608 | tf_op jit(solution)/shard_map/all_to_all | solution.py:53
  69.7 0.0 all-reduce.2.cloned.1.call-start
  69.8 50.2 %all-to-all-done = bf16[32,256,256]{2,1,0:T(8,128)(2,1)} async-done(((bf16[32,256,256]{2,1,0:T(8,128)(2,1)}), bf16[32,256,256]{2,1,0:T(8,128)(2,1)}, u32[]{:S(2)}, u32[]{:S(2)}) %all-to-all-start) | async-done | bytes 4194336 | tf_op jit(solution)/shard_map/all_to_all | solution.py:53
  119.9 10.2 %fusion.5 = f32[256,32,32]{2,1,0:T(8,128)} fusion(bf16[32,256,256]{2,1,0:T(8,128)(2,1)} %all-to-all-done), kind=kOutput, calls=%fused_computation.13 | convolution fusion | flops 134217728 | bytes 5242880 | tf_op jit(solution)/shard_map/fne,hne->nfh/dot_general | solution.py:18
  130.1 3.5 copy.33
  133.6 0.1 multiply_convert_fusion.5
  133.8 0.7 fusion.35
  134.5 0.4 fusion.20
  134.9 1.0 fusion.16
  135.9 0.6 fusion.12
  136.5 3.0 copy.37
  139.5 4.9 fusion.2
  144.5 2.4 copy.38
  146.9 57.9 %all_to_all.10 = bf16[32,256,256]{2,1,0:T(8,128)(2,1)} all-to-all(bf16[32,256,256]{2,1,0:T(8,128)(2,1)S(1)} %copy.38), channel_id=1, replica_groups=mesh['feat'=32,'samp'=8] {'feat'}, dimensions={0} | all-to-all | bytes 8388608 | tf_op jit(solution)/shard_map/all_to_all | solution.py:55
  204.8 40.9 %scatter_custom_fusion = f32[768,256]{1,0:T(8,128)S(1)} fusion(s32[8192]{0:T(1024)} %bitcast.53, bf16[8192,256]{1,0:T(8,128)(2,1)} %bitcast.48, f32[]{:T(128)} %constant.16.clone.1), kind=kCustom, calls=%fused_computation.2 | custom fusion | flops 4194304 | bytes 4981248 | tf_op jit(solution)/shard_map/scatter-add | solution.py:56
  245.7 4.2 convolution_convert_fusion.1
  249.9 0.0 all-reduce.2.cloned.1.call-update
  250.0 0.0 all-gather.3.cloned.1.call-start
  250.0 10.2 %convolution_convert_fusion = bf16[1024,2048]{1,0:T(8,128)(2,1)} fusion(f32[768,2048]{1,0:T(8,128)} %get-tuple-element.4, bf16[1,2048,256]{2,1,0:T(8,128)(2,1)S(1)} %copy-done.6, s32[1,768,1024]{2,1,0:T(8,128)} %param.7, f32[768,256]{1,0:T(8,128)S(1)} %scatter_custom_fusion), kind=kOutput, calls=%fused_computation.12 | convolution fusion | flops 4046127104 | bytes 15466496 | tf_op jit(solution)/shard_map/rh,rk->hk/dot_general | solution.py:67
  260.2 61.5 %all-reduce.2.cloned.1.call-done = bf16[2048,256]{1,0:T(8,128)(2,1)} async-done(((bf16[2048,256]{1,0:T(8,128)(2,1)}), bf16[2048,256]{1,0:T(8,128)(2,1)}) %all-reduce.2.cloned.1.call-update) | async-done | bytes 1048592 | tf_op jit(solution)/shard_map/psum | solution.py:72
  321.7 1.6 convert_bitcast_fusion.1
  323.3 332.7 %all-gather.3.cloned.1.call-done = bf16[8192,2048]{1,0:T(8,128)(2,1)} async-done(((bf16[1024,2048]{1,0:T(8,128)(2,1)}), bf16[8192,2048]{1,0:T(8,128)(2,1)}) %all-gather.3.cloned.1.call-update) | async-done | bytes 33554448 | tf_op jit(solution)/shard_map/all_gather | solution.py:69
  656.0 14.3 %reduce_sum.12 = bf16[1024,2048]{1,0:T(8,128)(2,1)} reduce(bf16[8,1024,2048]{2,1,0:T(8,128)(2,1)} %bitcast.47, bf16[]{:T(256)} %constant.13.clone.1), dimensions={0}, to_apply=%region_1.2 | reduce | flops 14680064 | bytes 37748736 | tf_op jit(solution)/shard_map/reduce_sum | solution.py:69
  670.3 2.1 convert_bitcast_fusion
  (23 shorter events, 0.1 us)
Async XLA Ops:
  7.2 126.6 %copy-start = (bf16[1024,1024]{1,0:T(8,128)(2,1)S(1)}, bf16[1024,1024]{1,0:T(8,128)(2,1)}, u32[]{:S(2)}) copy-start(bf16[1024,1024]{1,0:T(8,128)(2,1)} %param.12) | copy-start | bytes 6291460
  10.2 11.5 %copy-start.5 = (bf16[1,2048,256]{2,1,0:T(8,128)(2,1)S(1)}, bf16[1,2048,256]{2,1,0:T(8,128)(2,1)}, u32[]{:S(2)}) copy-start(bf16[1,2048,256]{2,1,0:T(8,128)(2,1)} %param.11) | copy-start | bytes 3145732
  20.0 1.6 copy-start.7
  60.9 8.8 %copy-start.3 = (bf16[1024]{0:T(1024)(128)(2,1)S(1)}, bf16[1024]{0:T(1024)(128)(2,1)}, u32[]{:S(2)}) copy-start(bf16[1024]{0:T(1024)(128)(2,1)} %param.13) | copy-start | bytes 6148
  60.9 8.9 %copy-start.4 = (s32[256,1]{0,1:T(1,128)S(1)}, s32[256,1]{0,1:T(1,128)}, u32[]{:S(2)}) copy-start(s32[256,1]{0,1:T(1,128)} %param.9) | copy-start | bytes 3076
  60.9 59.0 %all-to-all-start = ((bf16[32,256,256]{2,1,0:T(8,128)(2,1)}), bf16[32,256,256]{2,1,0:T(8,128)(2,1)}, u32[]{:S(2)}, u32[]{:S(2)}) async-start(bf16[32,256,256]{2,1,0:T(8,128)(2,1)} %broadcast_select_fusion), calls=%async_computation | async-start | bytes 8388608 | tf_op jit(solution)/shard_map/all_to_all | solution.py:53
  69.7 252.0 %all-reduce.2.cloned.1.call-start = ((), (), s32[]{:S(2)}) async-start(), calls=%async_computation.2 | async-start | bytes 2097152 | tf_op jit(solution)/shard_map/psum | solution.py:72
  245.7 4.3 copy-start.2
  245.7 4.3 copy-start.6
  250.0 406.0 %all-gather.3.cloned.1.call-start = ((), (), s32[]{:S(2)}) async-start(), calls=%async_computation.3 | async-start | bytes 37748736 | tf_op jit(solution)/shard_map/all_gather | solution.py:69
  656.0 16.4 %copy-start.1 = (bf16[1024,1024]{1,0:T(8,128)(2,1)S(1)}, bf16[1024,1024]{1,0:T(8,128)(2,1)}, u32[]{:S(2)}) copy-start(bf16[1024,1024]{1,0:T(8,128)(2,1)} %param.12) | copy-start | bytes 6291460
Sparse Core Ops, SparseCore 0:
  250.1 71.5 all-reduce.1
  323.5 332.4 all-gather.2
